TPU v7x, 512 devices: a whole 4x4x16 slice. The times are simulated.
512 devices in a mesh: dp: 4 (over y), expert: 128 (over x, z, core).
Axes of the slice: x: 4, y: 4, z: 16, core: 2. Of those that a mesh axis runs over, the one named last changes fastest.
Arguments:
- tokens: bfloat16 [12288, 2048], P(('dp', 'expert')), may hold values from -6 to 6
- cotangent: bfloat16 [12288, 2048], P(('dp', 'expert')), may hold values from -6 to 6
- routes: int32 [12288, 8], P(('dp', 'expert')), may hold values from 0 to 127, all different within a row; in each aligned block of 24 rows (0 to 23, 24 to 47, ...) at most 2 rows name the same one
- gates: bfloat16 [12288, 8], P(('dp', 'expert')), may hold values from 0.029907227 to 0.25
- plan: int32 [128], replicated, may hold values from 0 to 127, as said below
- gate_values: bfloat16 [128, 768, 2048], P('expert', 'dp'), may hold values from -0.125 to 0.125
- up_values: bfloat16 [128, 768, 2048], P('expert', 'dp'), may hold values from -0.125 to 0.125
- down_values: bfloat16 [128, 768, 2048], P('expert', 'dp'), may hold values from -0.21875 to 0.21875
- gate_scales: float32 [128, 12, 16], P('expert', 'dp'), may hold values from 0.5 to 2
- up_scales: float32 [128, 12, 16], P('expert', 'dp'), may hold values from 0.5 to 2
- down_scales: float32 [128, 12, 16], P('expert', 'dp'), may hold values from 0.5 to 2
Outputs:
- token_grads: bfloat16 [12288, 2048], P(('dp', 'expert'))
- gate_grads: bfloat16 [128, 768, 2048], P('expert', 'dp')
- up_grads: bfloat16 [128, 768, 2048], P('expert', 'dp')
- down_grads: bfloat16 [128, 768, 2048], P('expert', 'dp')
Inputs may be any that keep to these rules, and one draw needn't show every extreme that they name: `routes`: each token names 8 different experts. Among the 24 tokens of one device no expert is named more than 2 times, and in every draw the tokens of some device name some expert exactly 2 times. plan[plan[s]] = s, and plan[s] is either s or (s + 64) % 128; plan[0] = 64.
All inputs are finite; a program needn't handle non-finite values.
Results may differ from a plain program's by a relative error of at most 0.0082.
Values may be sent and summed in bfloat16 or wider, within the bound.
No kernel may reach another device: no remote copies, remote signals or barrier semaphores. Data moves between devices by JAX's collectives and lax.ppermute only.
A program may use at most 128 MiB of HBM per device.

v0:
```python
import jax
import jax.numpy as jnp
from jax import lax
from jax.sharding import PartitionSpec as P


def swapped(block, axis, stride):
    count = lax.axis_size(axis)
    route = []
    for low in range(count):
        high = low | 1 << stride
        if high != low and high < count:
            route += [(low, high), (high, low)]
    return lax.ppermute(block, axis, route)


def dequantize(values, scales):
    row_block = values.shape[0] // scales.shape[0]
    col_block = values.shape[1] // scales.shape[1]
    spread = jnp.repeat(jnp.repeat(scales, row_block, axis=0), col_block, axis=1)
    return (values.astype(jnp.float32) * spread).astype(jnp.bfloat16)


def slot_choice(route_lists, experts, capacity):
    numbers = jnp.arange(experts, dtype=jnp.int32)
    flattened = route_lists.reshape(-1)
    marked = (flattened[:, None] == numbers).astype(jnp.int32)
    slot_index = jnp.sum((jnp.cumsum(marked, axis=0) - 1) * marked, axis=-1)
    position = flattened * capacity + slot_index
    selected = position[:, None] == jnp.arange(experts * capacity, dtype=jnp.int32)
    return selected.reshape(route_lists.shape + (experts * capacity,))


def contract(left, right, left_dim, right_dim):
    return lax.dot_general(
        left, right, (((left_dim,), (right_dim,)), ((), ())), preferred_element_type=jnp.float32
    )


def expert_work(token_rows, cot_rows, w_gate, w_up, w_down):
    pre_gate = contract(token_rows, w_gate, 1, 1)
    pre_up = contract(token_rows, w_up, 1, 1)
    sigmoid_gate = jax.nn.sigmoid(pre_gate)
    activated = pre_gate * sigmoid_gate
    hidden = (activated * pre_up).astype(jnp.bfloat16)
    grad_hidden = contract(cot_rows, w_down, 1, 1)
    grad_gate = (
        grad_hidden * pre_up * sigmoid_gate * (1.0 + pre_gate * (1.0 - sigmoid_gate))
    ).astype(jnp.bfloat16)
    grad_up = (grad_hidden * activated).astype(jnp.bfloat16)
    gate_grad = contract(grad_gate, token_rows, 0, 0).astype(jnp.bfloat16)
    up_grad = contract(grad_up, token_rows, 0, 0).astype(jnp.bfloat16)
    down_grad = contract(hidden, cot_rows, 0, 0).astype(jnp.bfloat16)
    row_grads = (
        jnp.dot(grad_gate, w_gate, preferred_element_type=jnp.float32)
        + jnp.dot(grad_up, w_up, preferred_element_type=jnp.float32)
    ).astype(jnp.bfloat16)
    return (row_grads, gate_grad, up_grad, down_grad)


def on_device(
    tokens,
    cotangent,
    routes,
    gates,
    plan,
    gate_values,
    up_values,
    down_values,
    gate_scales,
    up_scales,
    down_scales,
):
    tok_count, features = tokens.shape
    experts = lax.axis_size("expert")
    replicas = lax.axis_size("dp")
    capacity = 2
    half_bit = experts.bit_length() - 2
    expert_index = lax.axis_index("expert")
    numbers = jnp.arange(experts, dtype=jnp.int32)
    is_moved = jnp.sum(jnp.where(numbers == expert_index, plan, 0)) != expert_index
    w_gate = dequantize(gate_values[0], gate_scales[0])
    w_up = dequantize(up_values[0], up_scales[0])
    w_down = dequantize(down_values[0], down_scales[0])
    selected = slot_choice(routes, experts, capacity)
    dispatch = (
        jnp.sum(selected.astype(jnp.int32), axis=1)
        .reshape(tok_count, experts, capacity)
        .astype(jnp.bfloat16)
    )
    outgoing = jnp.einsum(
        "rec,rd->ecd", dispatch, tokens, preferred_element_type=jnp.float32
    ).astype(jnp.bfloat16)
    slot_gate = jnp.einsum(
        "rkx,rk->x", selected.astype(jnp.float32), gates.astype(jnp.float32)
    ).reshape(experts, capacity)
    lifted = jnp.einsum("rec,rd->ecd", dispatch, cotangent, preferred_element_type=jnp.float32)
    cot_out = (lifted * slot_gate[..., None]).astype(jnp.bfloat16)
    both = jnp.stack([outgoing, cot_out], axis=0)
    arrived = lax.all_to_all(both, "expert", split_axis=1, concat_axis=1, tiled=True)
    gathered = lax.all_gather(arrived, "dp", axis=1, tiled=True)
    token_rows = gathered[0].reshape(-1, features)
    cot_rows = gathered[1].reshape(-1, features)
    row_grads, gate_grad, up_grad, down_grad = expert_work(
        token_rows, cot_rows, w_gate, w_up, w_down
    )
    summed_rows = lax.psum_scatter(
        row_grads.reshape(replicas, experts, capacity, features),
        "dp",
        scatter_dimension=0,
        tiled=True,
    )
    returned = lax.all_to_all(summed_rows[0], "expert", split_axis=0, concat_axis=0, tiled=True)
    token_grads = jnp.einsum(
        "rec,ecd->rd", dispatch, returned, preferred_element_type=jnp.float32
    ).astype(jnp.bfloat16)
    arrived_grads = swapped((gate_grad, up_grad, down_grad), "expert", half_bit)
    gate_grad = jnp.where(is_moved, arrived_grads[0], gate_grad)
    up_grad = jnp.where(is_moved, arrived_grads[1], up_grad)
    down_grad = jnp.where(is_moved, arrived_grads[2], down_grad)
    return (token_grads, gate_grad[None], up_grad[None], down_grad[None])


def solution(mesh):
    return jax.shard_map(
        on_device,
        mesh=mesh,
        in_specs=(
            P(("dp", "expert"), None),
            P(("dp", "expert"), None),
            P(("dp", "expert"), None),
            P(("dp", "expert"), None),
            P(),
            P("expert", "dp", None),
            P("expert", "dp", None),
            P("expert", "dp", None),
            P("expert", "dp", None),
            P("expert", "dp", None),
            P("expert", "dp", None),
        ),
        out_specs=(
            P(("dp", "expert"), None),
            P("expert", "dp", None),
            P("expert", "dp", None),
            P("expert", "dp", None),
        ),
        check_vma=False,
    )
```

profile of v0, /device:TPU:1, one launch (start us, length us, event | category | flops | bytes accessed | tf_op | source)
XLA Modules:
  0.0 426.3 jit_solution(17713711811344199833)
XLA Ops:
  7.3 0.8 copy.50
  8.0 0.1 eq.62
  8.1 0.1 iota_compare_fusion.1
  8.3 0.1 fusion.26
  8.5 0.2 fusion.29
  8.7 0.1 reduce_sum.30
  8.8 0.1 convert_reduce_fusion
  8.9 0.1 copy.54
  9.1 0.1 copy.61
  9.1 0.1 copy.57
  9.2 0.7 bitcast_convert_fusion
  9.9 0.7 select_reduce_fusion
  10.6 0.1 copy.69
  10.7 0.5 fusion.2
  11.2 0.5 fusion.1
  11.6 0.2 pad_maximum_fusion
  11.9 2.2 copy.58
  14.0 119.5 %all_to_all.10 = bf16[2,128,2,2048]{3,2,0,1:T(2,128)(2,1)} all-to-all(bf16[2,128,2,2048]{3,2,0,1:T(2,128)(2,1)S(1)} %copy.58), channel_id=1, replica_groups=mesh['dp'=4,'expert'=128] {'expert'}, dimensions={1} | all-to-all | bytes 4194304 | tf_op jit(solution)/shard_map/all_to_all | solution.py:100
  133.5 0.0 reduce-scatter.2.cloned.1.call-start
  133.6 0.6 copy-done.9
  134.2 0.5 copy-done.4
  134.7 0.2 convert_bitcast_fusion.1
  134.9 0.3 copy.78
  135.2 0.4 copy-done.10
  135.5 0.5 copy-done.5
  136.0 0.2 convert_bitcast_fusion.3
  136.2 0.3 copy.76
  136.5 0.8 copy-done.6
  137.3 0.2 convert_bitcast_fusion.4
  137.5 0.3 copy.74
  137.8 0.4 copy-done.11
  138.2 0.5 fusion.8
  138.7 1.4 fusion.9
  140.1 0.5 fusion.10
  140.6 77.3 %all-gather.2.cloned.1.call-done = bf16[2,512,2,2048]{3,2,0,1:T(2,128)(2,1)} async-done(((bf16[2,128,2,2048]{3,2,0,1:T(2,128)(2,1)}), bf16[2,512,2,2048]{3,2,0,1:T(2,128)(2,1)}) %all-gather.2.cloned.1.call-update) | async-done | bytes 8388624 | tf_op jit(solution)/shard_map/all_gather | solution.py:101
  217.9 8.4 %fusion.34 = (bf16[1,512,2,2048]{3,2,0,1:T(2,128)(2,1)}, bf16[1,512,2,2048]{3,2,0,1:T(2,128)(2,1)}) fusion(bf16[2,512,2,2048]{3,2,0,1:T(2,128)(2,1)} %all-gather.2.cloned.1.call-done), kind=kLoop, calls=%fused_computation.70 | loop fusion | bytes 16777216 | tf_op jit(solution)/shard_map/slice | solution.py:103
  226.3 7.2 %reshape_squeeze.7 = bf16[1024,2048]{1,0:T(8,128)(2,1)} reshape(bf16[1,512,2,2048]{3,2,0,1:T(2,128)(2,1)} %get-tuple-element.5) | data formatting | bytes 8388608 | tf_op jit(solution)/shard_map/reshape;squeeze | solution.py:102
  233.5 4.8 %fusion.15 = f32[1024,192]{0,1:T(8,128)} fusion(bf16[1024,2048]{1,0:T(8,128)(2,1)} %reshape_squeeze.7, bf16[24,8,16,128]{3,2,1,0:T(8,128)(2,1)S(1)} %bitcast.130), kind=kOutput, calls=%fused_computation.30 | convolution fusion | flops 805306368 | bytes 5767168 | tf_op jit(solution)/shard_map/dot_general | solution.py:35
  238.2 2.4 fusion.18
  240.7 7.2 %reshape_squeeze.6 = bf16[1024,2048]{1,0:T(8,128)(2,1)} reshape(bf16[1,512,2,2048]{3,2,0,1:T(2,128)(2,1)} %get-tuple-element.4) | data formatting | bytes 8388608 | tf_op jit(solution)/shard_map/reshape;squeeze | solution.py:103
  247.9 4.3 %multiply_convert_fusion.1 = (bf16[1024,192]{0,1:T(8,128)(2,1)S(1)}, bf16[1024,192]{0,1:T(8,128)(2,1)S(1)}) fusion(f32[1024,192]{0,1:T(8,128)} %fusion.15, f32[1024,192]{0,1:T(8,128)} %fusion.18, bf16[1024,2048]{1,0:T(8,128)(2,1)} %reshape_squeeze.6, bf16[24,8,16,128]{3,2,1,0:T(8,128)(2,1)S(1)} %bitcast.129), kind=kOutput, calls=%fused_computation.43 | convolution fusion | flops 807862272 | bytes 7340032 | tf_op jit(solution)/shard_map/dot_general | solution.py:35
  252.2 0.5 broadcast_in_dim.39
  252.7 1.4 fusion.12
  254.1 0.5 broadcast_in_dim.37
  254.5 3.4 add_convert_fusion
  258.0 7.7 %reshape.126 = bf16[4,128,2,2048]{3,2,1,0:T(2,128)(2,1)} reshape(bf16[1024,2048]{1,0:T(8,128)(2,1)} %add_convert_fusion) | data formatting | bytes 8388608 | tf_op jit(solution)/shard_map/reshape | solution.py:108
  265.6 6.0 %copy.59 = bf16[4,128,2,2048]{3,1,2,0:T(8,128)(2,1)} copy(bf16[4,128,2,2048]{3,2,1,0:T(2,128)(2,1)} %reshape.126) | data formatting | bytes 8388608 | tf_op jit(solution)/shard_map/reshape | solution.py:108
  271.7 55.8 %reduce-scatter.2.cloned.1.call-done = bf16[1,128,2,2048]{3,1,2,0:T(8,128)(2,1)} async-done(((bf16[4,128,2,2048]{3,1,2,0:T(8,128)(2,1)}), bf16[1,128,2,2048]{3,1,2,0:T(8,128)(2,1)}) %reduce-scatter.2.cloned.1.call-update) | async-done | bytes 1048592 | tf_op jit(solution)/shard_map/reduce_scatter | solution.py:107
  327.5 3.3 copy.60
  330.8 16.9 %all-to-all-start.1 = ((bf16[128,2,2048]{2,1,0:T(2,128)(2,1)}), bf16[128,2,2048]{2,1,0:T(2,128)(2,1)S(1)}, u32[]{:S(2)}, u32[]{:S(2)}) async-start(bf16[128,2,2048]{2,1,0:T(2,128)(2,1)} %copy.60), calls=%async_computation.2 | async-start | bytes 2097152 | tf_op jit(solution)/shard_map/all_to_all | solution.py:113
  347.7 3.7 convolution_convert_fusion.1
  351.4 5.1 %collective-permute-start.2 = (bf16[192,2048]{1,0:T(8,128)(2,1)S(1)}, bf16[192,2048]{1,0:T(8,128)(2,1)}, u32[]{:S(2)}, u32[]{:S(2)}) collective-permute-start(bf16[192,2048]{1,0:T(8,128)(2,1)S(1)} %convolution_convert_fusion.1), channel_id=1, source_target_pairs={{0,64},{64,0},{1,65},{65,1},{2,66},{66,2},{3,67},{67,3},{4,68},{68... | collective-permute-start | bytes 2359304 | tf_op jit(solution)/shard_map/ppermute | solution.py:14
  356.5 0.6 fusion.32
  357.8 3.3 convolution_convert_fusion.2
  361.2 1.9 collective-permute-start.1
  363.1 1.0 convolution_convert_fusion.3
  364.1 4.9 %collective-permute-start = (bf16[192,2048]{1,0:T(8,128)(2,1)S(1)}, bf16[192,2048]{1,0:T(8,128)(2,1)S(1)}, u32[]{:S(2)}, u32[]{:S(2)}) collective-permute-start(bf16[192,2048]{1,0:T(8,128)(2,1)S(1)} %convolution_convert_fusion.3), channel_id=1, source_target_pairs={{0,64},{64,0},{1,65},{65,1},{2,66},{66,2},{3,67},{67,3},{4,68},{68... | collective-permute-start | bytes 2359304 | tf_op jit(solution)/shard_map/ppermute | solution.py:14
  369.0 9.6 %collective-permute-done.2 = bf16[192,2048]{1,0:T(8,128)(2,1)} collective-permute-done((bf16[192,2048]{1,0:T(8,128)(2,1)S(1)}, bf16[192,2048]{1,0:T(8,128)(2,1)}, u32[]{:S(2)}, u32[]{:S(2)}) %collective-permute-start.2) | collective-permute-done | bytes 786464 | tf_op jit(solution)/shard_map/ppermute | solution.py:14
  378.6 1.0 select_bitcast_fusion
  379.6 20.6 %collective-permute-done.1 = bf16[192,2048]{1,0:T(8,128)(2,1)S(1)} collective-permute-done((bf16[192,2048]{1,0:T(8,128)(2,1)S(1)}, bf16[192,2048]{1,0:T(8,128)(2,1)S(1)}, u32[]{:S(2)}, u32[]{:S(2)}) %collective-permute-start.1) | collective-permute-done | bytes 786464 | tf_op jit(solution)/shard_map/ppermute | solution.py:14
  400.2 1.0 select_bitcast_fusion.1
  401.1 16.1 %collective-permute-done = bf16[192,2048]{1,0:T(8,128)(2,1)S(1)} collective-permute-done((bf16[192,2048]{1,0:T(8,128)(2,1)S(1)}, bf16[192,2048]{1,0:T(8,128)(2,1)S(1)}, u32[]{:S(2)}, u32[]{:S(2)}) %collective-permute-start) | collective-permute-done | bytes 786464 | tf_op jit(solution)/shard_map/ppermute | solution.py:14
  417.2 1.0 select_bitcast_fusion.2
  418.2 1.3 fusion.3
  (40 shorter events, 0.3 us)
Async XLA Ops:
  7.2 3.5 copy-start
  7.2 4.0 copy-start.8
  7.2 210.7 %all-gather.2.cloned.1.call-start = ((), (), s32[]{:S(2)}) async-start(), calls=%async_computation.3 | async-start | bytes 10485760 | tf_op jit(solution)/shard_map/all_gather | solution.py:101
  133.5 0.7 copy-start.9
  133.5 1.1 copy-start.4
  133.5 193.9 %reduce-scatter.2.cloned.1.call-start = ((), (), s32[]{:S(2)}) async-start(), calls=%async_computation.4 | async-start | bytes 5242880 | tf_op jit(solution)/shard_map/reduce_scatter | solution.py:107
  134.8 0.7 copy-start.10
  134.9 1.1 copy-start.5
  136.2 1.1 copy-start.6
  137.5 0.7 copy-start.11
  233.5 4.8 %copy-start.2 = (bf16[1024,2048]{1,0:T(8,128)(2,1)S(1)}, bf16[1024,2048]{1,0:T(8,128)(2,1)}, u32[]{:S(2)}) copy-start(bf16[1024,2048]{1,0:T(8,128)(2,1)} %reshape_squeeze.7) | copy-start | bytes 12582916
  233.5 4.8 %copy-start.7 = (bf16[192,16,128]{2,1,0:T(8,128)(2,1)S(1)}, bf16[192,16,128]{2,1,0:T(8,128)(2,1)}, u32[]{:S(2)}) copy-start(bf16[192,16,128]{2,1,0:T(8,128)(2,1)} %fusion.9) | copy-start | bytes 2359300
  330.8 87.4 %all-to-all-start.1 = ((bf16[128,2,2048]{2,1,0:T(2,128)(2,1)}), bf16[128,2,2048]{2,1,0:T(2,128)(2,1)S(1)}, u32[]{:S(2)}, u32[]{:S(2)}) async-start(bf16[128,2,2048]{2,1,0:T(2,128)(2,1)} %copy.60), calls=%async_computation.2 | async-start | bytes 2097152 | tf_op jit(solution)/shard_map/all_to_all | solution.py:113
  347.7 8.8 %copy-start.12 = (s32[128]{0:T(128)S(1)}, s32[128]{0:T(128)}, u32[]{:S(2)}) copy-start(s32[128]{0:T(128)} %param.15) | copy-start | bytes 1540
  351.4 27.2 %collective-permute-start.2 = (bf16[192,2048]{1,0:T(8,128)(2,1)S(1)}, bf16[192,2048]{1,0:T(8,128)(2,1)}, u32[]{:S(2)}, u32[]{:S(2)}) collective-permute-start(bf16[192,2048]{1,0:T(8,128)(2,1)S(1)} %convolution_convert_fusion.1), channel_id=1, source_target_pairs={{0,64},{64,0},{1,65},{65,1},{2,66},{66,2},{3,67},{67,3},{4,68},{68... | collective-permute-start | bytes 2359304 | tf_op jit(solution)/shard_map/ppermute | solution.py:14
  357.8 5.3 %copy-start.3 = (bf16[1024,2048]{1,0:T(8,128)(2,1)S(1)}, bf16[1024,2048]{1,0:T(8,128)(2,1)}, u32[]{:S(2)}) copy-start(bf16[1024,2048]{1,0:T(8,128)(2,1)} %reshape_squeeze.7) | copy-start | bytes 12582916
  361.2 39.0 %collective-permute-start.1 = (bf16[192,2048]{1,0:T(8,128)(2,1)S(1)}, bf16[192,2048]{1,0:T(8,128)(2,1)S(1)}, u32[]{:S(2)}, u32[]{:S(2)}) collective-permute-start(bf16[192,2048]{1,0:T(8,128)(2,1)S(1)} %convolution_convert_fusion.2), channel_id=1, source_target_pairs={{0,64},{64,0},{1,65},{65,1},{2,66},{66,2},{3,67},{67,3},{4,68},{68... | collective-permute-start | bytes 2359304 | tf_op jit(solution)/shard_map/ppermute | solution.py:14
  364.1 53.1 %collective-permute-start = (bf16[192,2048]{1,0:T(8,128)(2,1)S(1)}, bf16[192,2048]{1,0:T(8,128)(2,1)S(1)}, u32[]{:S(2)}, u32[]{:S(2)}) collective-permute-start(bf16[192,2048]{1,0:T(8,128)(2,1)S(1)} %convolution_convert_fusion.3), channel_id=1, source_target_pairs={{0,64},{64,0},{1,65},{65,1},{2,66},{66,2},{3,67},{67,3},{4,68},{68... | collective-permute-start | bytes 2359304 | tf_op jit(solution)/shard_map/ppermute | solution.py:14
  400.2 19.3 %copy-start.1 = (bf16[24,2048]{1,0:T(8,128)(2,1)S(1)}, bf16[24,2048]{1,0:T(8,128)(2,1)}, u32[]{:S(2)}) copy-start(bf16[24,2048]{1,0:T(8,128)(2,1)} %param.11) | copy-start | bytes 294916
Sparse Core Ops, SparseCore 0:
  133.7 84.1 all-gather.1
  271.8 55.6 reduce-scatter.1
where the time goes:
time: 427 us; the launch traced here: 426 us
  waiting for transfers between devices  179 us (42%)
  blocking collectives  119 us (28%)
  local copies, waits for them, and re-layouts  48.3 us (11%)
  starting transfers between devices  28.9 us (7%)
  matrix products  26.6 us (6%)
  between operations  15 us (4%)
  other arithmetic  8.66 us (2%)
    all_to_all x1, blocking collectives, on_device(): lax.all_to_all(both, 'expert', split_axis=1, concat_axis=1, tiled=True)  119 us
    all_gather x1, waiting for transfers between devices, on_device(): gathered = lax.all_gather(arrived, 'dp', axis=1, tiled=True)  77.3 us
    reduce_scatter x1, waiting for transfers between devices, on_device(): lax.psum_scatter(row_grads.reshape(replicas, experts, capacity, features)...  55.8 us
    ppermute x3, waiting for transfers between devices, swapped(): return lax.ppermute(block, axis, route)  46.3 us
    dot_general x6, matrix products, contract(): lax.dot_general(left, right, (((left_dim,), (right_dim,)), ((), ())), pre...  19.5 us
    all_to_all x1, starting transfers between devices, on_device(): lax.all_to_all(summed_rows[0], 'expert', split_axis=0, concat_axis=0, til...  16.9 us
    reshape x2, local copies, waits for them, and re-layouts, on_device(): row_grads.reshape(replicas, experts, capacity, features)  13.7 us
    ppermute x3, starting transfers between devices, swapped(): return lax.ppermute(block, axis, route)  11.9 us
  transfers between devices with their start and end apart: 6, of which 5 were waited for; matrix products, arithmetic and copies ran while one was open for 4% of the time, Pallas kernels for 0%

commit v1 on v0

--- a/solution.py
+++ b/solution.py
@@ -98,7 +98,25 @@
     cot_out = (lifted * slot_gate[..., None]).astype(jnp.bfloat16)
     both = jnp.stack([outgoing, cot_out], axis=0)
     arrived = lax.all_to_all(both, "expert", split_axis=1, concat_axis=1, tiled=True)
-    gathered = lax.all_gather(arrived, "dp", axis=1, tiled=True)
+    kept_arr, latest, mixed_arr = (lax.axis_size("dp"), lax.axis_index("dp"), arrived.shape[1])
+    slots = tuple(((rr, (rr + 1) % kept_arr) for rr in range(kept_arr)))
+    kept_rows = tuple(((rr, (rr - 1) % kept_arr) for rr in range(kept_arr)))
+    gathered = jnp.zeros(
+        (*arrived.shape[:1], kept_arr * mixed_arr, *arrived.shape[2:]), arrived.dtype
+    )
+    gathered = lax.dynamic_update_slice_in_dim(gathered, arrived, latest * mixed_arr, axis=1)
+    w2 = block_out = arrived
+    aux = kept_arr // 2
+    for q in [*range(1, aux + 1)]:
+        w2 = lax.ppermute(w2, "dp", slots)
+        gathered = lax.dynamic_update_slice_in_dim(
+            gathered, w2, (latest - q) % kept_arr * mixed_arr, axis=1
+        )
+        if q < kept_arr - aux:
+            block_out = lax.ppermute(block_out, "dp", kept_rows)
+            gathered = lax.dynamic_update_slice_in_dim(
+                gathered, block_out, (latest + q) % kept_arr * mixed_arr, axis=1
+            )
     token_rows = gathered[0].reshape(-1, features)
     cot_rows = gathered[1].reshape(-1, features)
     row_grads, gate_grad, up_grad, down_grad = expert_work(

time: 427 us -> 436 us (1.021)
  waiting for transfers between devices: 179 us -> 160 us
  local copies, waits for them, and re-layouts: 48.3 us -> 63 us
  starting transfers between devices: 28.9 us -> 37.5 us
    all_gather x1 -> x0, waiting for transfers between devices: 77.3 us -> none  [on_device(): gathered = lax.all_gather(arrived, 'dp', axis=1, tiled=True)]
    ppermute x0 -> x3, waiting for transfers between devices: none -> 67 us  [the longest x2 67 us: on_device(): w2 = lax.ppermute(w2, 'dp', slots)]
    dynamic_update_slice x0 -> x4, local copies, waits for them, and re-layouts: none -> 11.1 us  [the longest x2 6.33 us: on_device(): lax.dynamic_update_slice_in_dim(gathered, w2, (latest - q) % kept_arr * m...]
    reduce_scatter x1, waiting for transfers between devices: 55.8 us -> 46.9 us  [on_device(): lax.psum_scatter(row_grads.reshape(replicas, experts, capacity, features)...]
    ppermute x0 -> x3, starting transfers between devices: none -> 8.63 us  [the longest x2 5.28 us: on_device(): w2 = lax.ppermute(w2, 'dp', slots)]
    broadcast_in_dim x0 -> x1, local copies, waits for them, and re-layouts: none -> 4.55 us  [on_device(): jnp.zeros((*arrived.shape[:1], kept_arr * mixed_arr, *arrived.shape[2:]),...]
  transfers between devices with their start and end apart: 6 -> 8, of which waited for: 5 -> 6; matrix products, arithmetic and copies ran while one was open for 4% -> 8% of each run, Pallas kernels for 0% -> 0%
where the time goes in v1:
time: 436 us; the launch traced here: 434 us
  waiting for transfers between devices  160 us (37%)
  blocking collectives  119 us (27%)
  local copies, waits for them, and re-layouts  63 us (14%)
  starting transfers between devices  37.5 us (9%)
  matrix products  26.3 us (6%)
  between operations  15.2 us (3%)
  other arithmetic  13 us (3%)
    all_to_all x1, blocking collectives, on_device(): lax.all_to_all(both, 'expert', split_axis=1, concat_axis=1, tiled=True)  119 us
    ppermute x2, waiting for transfers between devices, on_device(): w2 = lax.ppermute(w2, 'dp', slots)  67 us
    reduce_scatter x1, waiting for transfers between devices, on_device(): lax.psum_scatter(row_grads.reshape(replicas, experts, capacity, features)...  46.9 us
    ppermute x3, waiting for transfers between devices, swapped(): return lax.ppermute(block, axis, route)  46 us
    dot_general x6, matrix products, contract(): lax.dot_general(left, right, (((left_dim,), (right_dim,)), ((), ())), pre...  19.3 us
    all_to_all x1, starting transfers between devices, on_device(): lax.all_to_all(summed_rows[0], 'expert', split_axis=0, concat_axis=0, til...  16.7 us
    reshape x2, local copies, waits for them, and re-layouts, on_device(): row_grads.reshape(replicas, experts, capacity, features)  13.7 us
    ppermute x3, starting transfers between devices, swapped(): return lax.ppermute(block, axis, route)  12.1 us
  transfers between devices with their start and end apart: 8, of which 6 were waited for; matrix products, arithmetic and copies ran while one was open for 8% of the time, Pallas kernels for 0%

profile of v1, /device:TPU:1, one launch (start us, length us, event | category | flops | bytes accessed | tf_op | source)
XLA Modules:
  0.0 434.4 jit_solution(13004930689010655251)
XLA Ops:
  7.3 0.8 copy.60
  8.0 0.1 eq.66
  8.1 0.1 iota_compare_fusion.1
  8.3 0.1 fusion.26
  8.5 0.2 fusion.29
  8.7 0.1 reduce_sum.30
  8.8 0.1 convert_reduce_fusion
  8.9 0.1 copy.64
  9.2 0.7 bitcast_convert_fusion
  9.9 0.7 select_reduce_fusion
  10.7 0.5 fusion.2
  11.2 0.5 fusion.1
  11.6 0.2 pad_maximum_fusion
  11.9 2.2 copy.68
  14.1 119.5 %all_to_all.10 = bf16[2,128,2,2048]{3,2,0,1:T(2,128)(2,1)S(1)} all-to-all(bf16[2,128,2,2048]{3,2,0,1:T(2,128)(2,1)S(1)} %copy.68), channel_id=1, replica_groups=mesh['dp'=4,'expert'=128] {'expert'}, dimensions={1} | all-to-all | bytes 4194304 | tf_op jit(solution)/shard_map/all_to_all | solution.py:100
  133.6 3.2 collective-permute-start
  136.8 0.2 convert_bitcast_fusion.1
  137.0 0.3 copy.92
  137.3 1.4 fusion.8
  138.7 3.3 collective-permute-start.1
  142.1 0.2 convert_bitcast_fusion.3
  142.3 0.3 copy.90
  142.6 1.4 fusion.9
  144.0 39.5 %collective-permute-done = bf16[2,128,2,2048]{3,2,0,1:T(2,128)(2,1)} collective-permute-done((bf16[2,128,2,2048]{3,2,0,1:T(2,128)(2,1)S(1)}, bf16[2,128,2,2048]{3,2,0,1:T(2,128)(2,1)}, u32[]{:S(2)}, u32[]{:S(2)}) %collective-permute-start) | collective-permute-done | bytes 2097184 | tf_op jit(solution)/shard_map/ppermute | solution.py:111
  183.5 2.1 collective-permute-start.2
  185.6 1.3 convert_bitcast_fusion.4
  186.9 2.9 copy.88
  189.9 2.8 fusion.10
  192.7 4.6 %broadcast_in_dim.37 = bf16[2,512,2,2048]{3,2,1,0:T(2,128)(2,1)S(1)} broadcast(bf16[]{:T(256)} %constant.46.clone.1), dimensions={} | broadcast | bytes 8388610 | tf_op jit(solution)/shard_map/broadcast_in_dim | solution.py:104
  197.3 1.6 copy_dynamic-update-slice_fusion.3
  198.8 3.2 copy_dynamic-update-slice_fusion.2
  202.0 3.2 copy_dynamic-update-slice_fusion.1
  205.2 27.5 %collective-permute-done.2 = bf16[2,128,2,2048]{3,2,0,1:T(2,128)(2,1)} collective-permute-done((bf16[2,128,2,2048]{3,2,0,1:T(2,128)(2,1)}, bf16[2,128,2,2048]{3,2,0,1:T(2,128)(2,1)}, u32[]{:S(2)}, u32[]{:S(2)}) %collective-permute-start.2) | collective-permute-done | bytes 2097184 | tf_op jit(solution)/shard_map/ppermute | solution.py:111
  232.7 3.2 copy_dynamic-update-slice_fusion
  235.9 7.0 %fusion.34 = (bf16[1,512,2,2048]{3,2,1,0:T(2,128)(2,1)}, bf16[1,512,2,2048]{3,2,1,0:T(2,128)(2,1)}) fusion(bf16[2,512,2,2048]{3,2,1,0:T(2,128)(2,1)S(1)} %copy_dynamic-update-slice_fusion), kind=kLoop, calls=%fused_computation.74 | loop fusion | bytes 16777216 | tf_op jit(solution)/shard_map/slice | solution.py:121
  242.9 7.3 %reshape_squeeze.7 = bf16[1024,2048]{1,0:T(8,128)(2,1)} reshape(bf16[1,512,2,2048]{3,2,1,0:T(2,128)(2,1)} %get-tuple-element.5) | data formatting | bytes 8388608 | tf_op jit(solution)/shard_map/reshape;squeeze | solution.py:120
  250.2 4.8 %fusion.15 = f32[1024,192]{0,1:T(8,128)} fusion(bf16[1024,2048]{1,0:T(8,128)(2,1)} %reshape_squeeze.7, bf16[24,8,16,128]{3,2,1,0:T(8,128)(2,1)S(1)} %bitcast.125), kind=kOutput, calls=%fused_computation.34 | convolution fusion | flops 805306368 | bytes 5767168 | tf_op jit(solution)/shard_map/dot_general | solution.py:35
  254.9 2.4 fusion.18
  257.4 7.3 %reshape_squeeze.6 = bf16[1024,2048]{1,0:T(8,128)(2,1)} reshape(bf16[1,512,2,2048]{3,2,1,0:T(2,128)(2,1)} %get-tuple-element.4) | data formatting | bytes 8388608 | tf_op jit(solution)/shard_map/reshape;squeeze | solution.py:121
  264.7 4.3 multiply_convert_fusion.1
  269.0 0.5 broadcast_in_dim.43
  269.5 1.4 fusion.12
  270.9 0.5 broadcast_in_dim.41
  271.3 0.7 copy-done.6
  272.0 3.4 add_convert_fusion
  275.4 7.7 %reshape.126 = bf16[4,128,2,2048]{3,2,1,0:T(2,128)(2,1)} reshape(bf16[1024,2048]{1,0:T(8,128)(2,1)} %add_convert_fusion) | data formatting | bytes 8388608 | tf_op jit(solution)/shard_map/reshape | solution.py:126
  283.0 6.0 %copy.73 = bf16[4,128,2,2048]{3,1,2,0:T(8,128)(2,1)} copy(bf16[4,128,2,2048]{3,2,1,0:T(2,128)(2,1)} %reshape.126) | data formatting | bytes 8388608 | tf_op jit(solution)/shard_map/reshape | solution.py:126
  289.0 46.9 %reduce-scatter.2.cloned.1.call-done = bf16[1,128,2,2048]{3,1,2,0:T(8,128)(2,1)} async-done(((bf16[4,128,2,2048]{3,1,2,0:T(8,128)(2,1)}), bf16[1,128,2,2048]{3,1,2,0:T(8,128)(2,1)}) %reduce-scatter.2.cloned.1.call-update) | async-done | bytes 1048592 | tf_op jit(solution)/shard_map/reduce_scatter | solution.py:125
  335.9 3.4 copy.74
  339.3 16.7 %all-to-all-start.1 = ((bf16[128,2,2048]{2,1,0:T(2,128)(2,1)}), bf16[128,2,2048]{2,1,0:T(2,128)(2,1)S(1)}, u32[]{:S(2)}, u32[]{:S(2)}) async-start(bf16[128,2,2048]{2,1,0:T(2,128)(2,1)} %copy.74), calls=%async_computation.2 | async-start | bytes 2097152 | tf_op jit(solution)/shard_map/all_to_all | solution.py:131
  356.1 3.5 convolution_convert_fusion.1
  359.5 5.3 %collective-permute-start.5 = (bf16[192,2048]{1,0:T(8,128)(2,1)S(1)}, bf16[192,2048]{1,0:T(8,128)(2,1)S(1)}, u32[]{:S(2)}, u32[]{:S(2)}) collective-permute-start(bf16[192,2048]{1,0:T(8,128)(2,1)S(1)} %convolution_convert_fusion.1), channel_id=1, source_target_pairs={{0,64},{64,0},{1,65},{65,1},{2,66},{66,2},{3,67},{67,3},{4,68},{68... | collective-permute-start | bytes 2359304 | tf_op jit(solution)/shard_map/ppermute | solution.py:14
  364.9 0.6 fusion.32
  366.2 3.3 convolution_convert_fusion.2
  369.5 1.9 collective-permute-start.4
  371.5 1.0 convolution_convert_fusion.3
  372.5 4.9 %collective-permute-start.3 = (bf16[192,2048]{1,0:T(8,128)(2,1)S(1)}, bf16[192,2048]{1,0:T(8,128)(2,1)S(1)}, u32[]{:S(2)}, u32[]{:S(2)}) collective-permute-start(bf16[192,2048]{1,0:T(8,128)(2,1)S(1)} %convolution_convert_fusion.3), channel_id=1, source_target_pairs={{0,64},{64,0},{1,65},{65,1},{2,66},{66,2},{3,67},{67,3},{4,68},{68... | collective-permute-start | bytes 2359304 | tf_op jit(solution)/shard_map/ppermute | solution.py:14
  377.4 9.4 %collective-permute-done.5 = bf16[192,2048]{1,0:T(8,128)(2,1)S(1)} collective-permute-done((bf16[192,2048]{1,0:T(8,128)(2,1)S(1)}, bf16[192,2048]{1,0:T(8,128)(2,1)S(1)}, u32[]{:S(2)}, u32[]{:S(2)}) %collective-permute-start.5) | collective-permute-done | bytes 786464 | tf_op jit(solution)/shard_map/ppermute | solution.py:14
  386.8 1.0 select_bitcast_fusion
  387.7 20.5 %collective-permute-done.4 = bf16[192,2048]{1,0:T(8,128)(2,1)S(1)} collective-permute-done((bf16[192,2048]{1,0:T(8,128)(2,1)S(1)}, bf16[192,2048]{1,0:T(8,128)(2,1)S(1)}, u32[]{:S(2)}, u32[]{:S(2)}) %collective-permute-start.4) | collective-permute-done | bytes 786464 | tf_op jit(solution)/shard_map/ppermute | solution.py:14
  408.2 1.0 select_bitcast_fusion.1
  409.2 16.1 %collective-permute-done.3 = bf16[192,2048]{1,0:T(8,128)(2,1)S(1)} collective-permute-done((bf16[192,2048]{1,0:T(8,128)(2,1)S(1)}, bf16[192,2048]{1,0:T(8,128)(2,1)S(1)}, u32[]{:S(2)}, u32[]{:S(2)}) %collective-permute-start.3) | collective-permute-done | bytes 786464 | tf_op jit(solution)/shard_map/ppermute | solution.py:14
  425.3 1.0 select_bitcast_fusion.2
  426.3 1.3 fusion.3
  (56 shorter events, 0.5 us)
Async XLA Ops:
  7.2 3.5 copy-start
  7.2 4.0 copy-start.11
  7.2 328.7 %reduce-scatter.2.cloned.1.call-start = ((), (), s32[]{:S(2)}) async-start(), calls=%async_computation.3 | async-start | bytes 5242880 | tf_op jit(solution)/shard_map/reduce_scatter | solution.py:125
  14.0 122.7 %copy-start.12 = (f32[1,3,16]{2,0,1:T(1,128)S(1)}, f32[1,3,16]{2,0,1:T(1,128)}, u32[]{:S(2)}) copy-start(f32[1,3,16]{2,0,1:T(1,128)} %param.19) | copy-start | bytes 580
  14.1 122.7 %copy-start.4 = (bf16[1,192,2048]{2,1,0:T(8,128)(2,1)S(1)}, bf16[1,192,2048]{2,1,0:T(8,128)(2,1)}, u32[]{:S(2)}) copy-start(bf16[1,192,2048]{2,1,0:T(8,128)(2,1)} %param.16) | copy-start | bytes 2359300
  133.6 49.9 %collective-permute-start = (bf16[2,128,2,2048]{3,2,0,1:T(2,128)(2,1)S(1)}, bf16[2,128,2,2048]{3,2,0,1:T(2,128)(2,1)}, u32[]{:S(2)}, u32[]{:S(2)}) collective-permute-start(bf16[2,128,2,2048]{3,2,0,1:T(2,128)(2,1)S(1)} %all_to_all.10), channel_id=1, source_target_pairs={{0,128},{128,256},{256,384},{384,0},{1,129},{129,257},{257,385},{3... | collective-permute-start | bytes 6291464 | tf_op jit(solution)/shard_map/ppermute | solution.py:111
  137.0 5.1 %copy-start.5 = (bf16[1,192,2048]{2,1,0:T(8,128)(2,1)S(1)}, bf16[1,192,2048]{2,1,0:T(8,128)(2,1)}, u32[]{:S(2)}) copy-start(bf16[1,192,2048]{2,1,0:T(8,128)(2,1)} %param.17) | copy-start | bytes 2359300
  137.3 4.9 %copy-start.13 = (f32[1,3,16]{2,0,1:T(1,128)S(1)}, f32[1,3,16]{2,0,1:T(1,128)}, u32[]{:S(2)}) copy-start(f32[1,3,16]{2,0,1:T(1,128)} %param.20) | copy-start | bytes 580
  138.7 63.3 %collective-permute-start.1 = (bf16[2,128,2,2048]{3,2,0,1:T(2,128)(2,1)S(1)}, bf16[2,128,2,2048]{3,2,0,1:T(2,128)(2,1)}, u32[]{:S(2)}, u32[]{:S(2)}) collective-permute-start(bf16[2,128,2,2048]{3,2,0,1:T(2,128)(2,1)S(1)} %all_to_all.10), channel_id=1, source_target_pairs={{0,384},{128,0},{256,128},{384,256},{1,385},{129,1},{257,129},{385... | collective-permute-start | bytes 6291464 | tf_op jit(solution)/shard_map/ppermute | solution.py:116
  142.3 43.3 %copy-start.7 = (bf16[1,192,2048]{2,1,0:T(8,128)(2,1)S(1)}, bf16[1,192,2048]{2,1,0:T(8,128)(2,1)}, u32[]{:S(2)}) copy-start(bf16[1,192,2048]{2,1,0:T(8,128)(2,1)} %param.18) | copy-start | bytes 2359300
  183.5 49.2 %collective-permute-start.2 = (bf16[2,128,2,2048]{3,2,0,1:T(2,128)(2,1)}, bf16[2,128,2,2048]{3,2,0,1:T(2,128)(2,1)}, u32[]{:S(2)}, u32[]{:S(2)}) collective-permute-start(bf16[2,128,2,2048]{3,2,0,1:T(2,128)(2,1)} %collective-permute-done), channel_id=1, source_target_pairs={{0,128},{128,256},{256,384},{384,0},{1,129},{129,257},{257,385},{3... | collective-permute-start | bytes 6291464 | tf_op jit(solution)/shard_map/ppermute | solution.py:111
  186.9 2.9 copy-start.14
  242.9 7.3 %copy-start.8 = (bf16[192,16,128]{2,1,0:T(8,128)(2,1)S(1)}, bf16[192,16,128]{2,1,0:T(8,128)(2,1)}, u32[]{:S(2)}) copy-start(bf16[192,16,128]{2,1,0:T(8,128)(2,1)} %fusion.8) | copy-start | bytes 2359300
  250.2 4.8 %copy-start.2 = (bf16[1024,2048]{1,0:T(8,128)(2,1)S(1)}, bf16[1024,2048]{1,0:T(8,128)(2,1)}, u32[]{:S(2)}) copy-start(bf16[1024,2048]{1,0:T(8,128)(2,1)} %reshape_squeeze.7) | copy-start | bytes 12582916
  250.2 4.8 %copy-start.9 = (bf16[192,16,128]{2,1,0:T(8,128)(2,1)S(1)}, bf16[192,16,128]{2,1,0:T(8,128)(2,1)}, u32[]{:S(2)}) copy-start(bf16[192,16,128]{2,1,0:T(8,128)(2,1)} %fusion.9) | copy-start | bytes 2359300
  257.4 7.3 %copy-start.10 = (bf16[192,16,128]{2,1,0:T(8,128)(2,1)S(1)}, bf16[192,16,128]{2,1,0:T(8,128)(2,1)}, u32[]{:S(2)}) copy-start(bf16[192,16,128]{2,1,0:T(8,128)(2,1)} %fusion.10) | copy-start | bytes 2359300
  270.8 1.1 copy-start.6
  335.9 20.1 %copy-start.16 = (f32[1024,192]{0,1:T(8,128)S(1)}, f32[1024,192]{0,1:T(8,128)}, u32[]{:S(2)}) copy-start(f32[1024,192]{0,1:T(8,128)} %fusion.15) | copy-start | bytes 2359300
  339.3 86.9 %all-to-all-start.1 = ((bf16[128,2,2048]{2,1,0:T(2,128)(2,1)}), bf16[128,2,2048]{2,1,0:T(2,128)(2,1)S(1)}, u32[]{:S(2)}, u32[]{:S(2)}) async-start(bf16[128,2,2048]{2,1,0:T(2,128)(2,1)} %copy.74), calls=%async_computation.2 | async-start | bytes 2097152 | tf_op jit(solution)/shard_map/all_to_all | solution.py:131
  356.0 8.8 %copy-start.15 = (s32[128]{0:T(128)S(1)}, s32[128]{0:T(128)}, u32[]{:S(2)}) copy-start(s32[128]{0:T(128)} %param.15) | copy-start | bytes 1540
  359.5 27.3 %collective-permute-start.5 = (bf16[192,2048]{1,0:T(8,128)(2,1)S(1)}, bf16[192,2048]{1,0:T(8,128)(2,1)S(1)}, u32[]{:S(2)}, u32[]{:S(2)}) collective-permute-start(bf16[192,2048]{1,0:T(8,128)(2,1)S(1)} %convolution_convert_fusion.1), channel_id=1, source_target_pairs={{0,64},{64,0},{1,65},{65,1},{2,66},{66,2},{3,67},{67,3},{4,68},{68... | collective-permute-start | bytes 2359304 | tf_op jit(solution)/shard_map/ppermute | solution.py:14
  366.2 5.3 %copy-start.3 = (bf16[1024,2048]{1,0:T(8,128)(2,1)S(1)}, bf16[1024,2048]{1,0:T(8,128)(2,1)}, u32[]{:S(2)}) copy-start(bf16[1024,2048]{1,0:T(8,128)(2,1)} %reshape_squeeze.7) | copy-start | bytes 12582916
  369.5 38.7 %collective-permute-start.4 = (bf16[192,2048]{1,0:T(8,128)(2,1)S(1)}, bf16[192,2048]{1,0:T(8,128)(2,1)S(1)}, u32[]{:S(2)}, u32[]{:S(2)}) collective-permute-start(bf16[192,2048]{1,0:T(8,128)(2,1)S(1)} %convolution_convert_fusion.2), channel_id=1, source_target_pairs={{0,64},{64,0},{1,65},{65,1},{2,66},{66,2},{3,67},{67,3},{4,68},{68... | collective-permute-start | bytes 2359304 | tf_op jit(solution)/shard_map/ppermute | solution.py:14
  372.5 52.8 %collective-permute-start.3 = (bf16[192,2048]{1,0:T(8,128)(2,1)S(1)}, bf16[192,2048]{1,0:T(8,128)(2,1)S(1)}, u32[]{:S(2)}, u32[]{:S(2)}) collective-permute-start(bf16[192,2048]{1,0:T(8,128)(2,1)S(1)} %convolution_convert_fusion.3), channel_id=1, source_target_pairs={{0,64},{64,0},{1,65},{65,1},{2,66},{66,2},{3,67},{67,3},{4,68},{68... | collective-permute-start | bytes 2359304 | tf_op jit(solution)/shard_map/ppermute | solution.py:14
  408.2 19.3 %copy-start.1 = (bf16[24,2048]{1,0:T(8,128)(2,1)S(1)}, bf16[24,2048]{1,0:T(8,128)(2,1)}, u32[]{:S(2)}) copy-start(bf16[24,2048]{1,0:T(8,128)(2,1)} %param.11) | copy-start | bytes 294916
Sparse Core Ops, SparseCore 0:
  289.2 46.6 reduce-scatter.1
